TPU v7x, 32 devices: a whole 2x2x4 slice. The times are simulated.
32 devices in a mesh: slab: 8 (over z, x), orient: 4 (over y, core).
Axes of the slice: x: 2, y: 2, z: 4, core: 2. Of those that a mesh axis runs over, the one named last changes fastest.
Arguments:
- tiles: bfloat16 [192, 1, 128, 128], P('slab'), may hold values from -8 to 8
- assigned_worker: int32 [192], P('slab'), may hold values from -1 to 7, as said below
- wedge_mask: int32 [128, 128], replicated, may hold values 0 or 1
- template_volume: float32 [64, 64, 64], replicated, may hold values from -6 to 6
- rotation_samples: int32 [64, 4096], P('orient', 'slab'), may hold values from 0 to 262143
Outputs:
- scores: bfloat16 [192, 128, 128], P('slab', 'orient')
Inputs may be any that keep to these rules, and one draw needn't show every extreme that they name: `assigned_worker`: the occupied slots of each slab index come first. Slab indices 2m and 2m+1 hold 24 occupied slots together, and some slab index has all 24 occupied. The occupied slots, taken in slot order over all slab indices, are dealt to the workers in turn, so every worker receives exactly 12 tiles and at most 3 from one slab index.
All inputs are finite; a program needn't handle non-finite values.
Results may differ from a plain program's by a relative error of at most 0.0085.
Values may be sent and summed in bfloat16 or wider, within the bound.
No kernel may reach another device: no remote copies, remote signals or barrier semaphores. Data moves between devices by JAX's collectives and lax.ppermute only.
A program may use at most 128 MiB of HBM per device.

v0:
```python
import math
import jax
import jax.numpy as jnp
from jax import lax
from jax.sharding import PartitionSpec as P


def partner(block, axis, bit):
    count = lax.axis_size(axis)
    route = []
    for low in range(count):
        high = low | 1 << bit
        if high != low and high < count:
            route += [(low, high), (high, low)]
    return lax.ppermute(block, axis, route)


def tables(length):
    counter = jnp.arange(length, dtype=jnp.int32)
    angles = (counter[:, None] * counter[None, :] % length).astype(jnp.float32) * (
        2.0 * math.pi / length
    )
    return (jnp.cos(angles).astype(jnp.bfloat16), jnp.sin(angles).astype(jnp.bfloat16))


def band_table(length, box_edge):
    counter = jnp.arange(length, dtype=jnp.int32)
    offsets = (counter[None, :] - counter[:, None]) % length
    return (offsets < box_edge).astype(jnp.float32)


def right_mul(values, table):
    return jnp.einsum("...ab,bc->...ac", values, table, preferred_element_type=jnp.float32)


def left_mul(table, values):
    return jnp.einsum("ka,...ab->...kb", table, values, preferred_element_type=jnp.float32)


def forward_two(values, cosine_table, sine_table):
    first_real = right_mul(values, cosine_table).astype(jnp.bfloat16)
    first_imag = (-right_mul(values, sine_table)).astype(jnp.bfloat16)
    second_real = (left_mul(cosine_table, first_real) + left_mul(sine_table, first_imag)).astype(
        jnp.bfloat16
    )
    second_imag = (left_mul(cosine_table, first_imag) - left_mul(sine_table, first_real)).astype(
        jnp.bfloat16
    )
    return (second_real, second_imag)


def inverse_real(real_part, imag_part, cosine_table, sine_table):
    length = real_part.shape[-1]
    first_real = (right_mul(real_part, cosine_table) - right_mul(imag_part, sine_table)).astype(
        jnp.bfloat16
    )
    first_imag = (right_mul(imag_part, cosine_table) + right_mul(real_part, sine_table)).astype(
        jnp.bfloat16
    )
    return (left_mul(cosine_table, first_real) - left_mul(sine_table, first_imag)) * (
        1.0 / (length * length)
    )


def filtered(values, wedge_weight, cosine_table, sine_table):
    spec_real, spec_imag = forward_two(values, cosine_table, sine_table)
    return inverse_real(
        spec_real * wedge_weight, spec_imag * wedge_weight, cosine_table, sine_table
    ).astype(jnp.bfloat16)


def pick_rows(chosen, source):
    counter = jnp.arange(source.shape[0], dtype=jnp.int32)
    selector = (chosen[:, None] == counter[None, :]).astype(source.dtype)
    flat = source.reshape(source.shape[0], -1)
    picked = jnp.dot(selector, flat, preferred_element_type=jnp.float32).astype(source.dtype)
    return picked.reshape((chosen.shape[0],) + source.shape[1:])


def make_templates(
    template_volume, rotation_samples, box_edge, planes, tile_len, cosine_table, sine_table
):
    count = rotation_samples.shape[0]
    sampled_part = jnp.take(template_volume.reshape(-1), rotation_samples, axis=0).astype(
        jnp.bfloat16
    )
    sampled = lax.all_gather(sampled_part, "slab", axis=1, tiled=True)
    sampled = sampled.reshape(count, planes, box_edge, box_edge)
    padded = jnp.pad(sampled, ((0, 0), (0, 0), (0, tile_len - box_edge), (0, tile_len - box_edge)))
    template_norm = jnp.sqrt(
        jnp.sum(jnp.square(sampled.astype(jnp.float32)), axis=(1, 2, 3)) + 1e-05
    )
    spec_real, spec_imag = forward_two(padded, cosine_table, sine_table)
    return (spec_real, spec_imag, template_norm)


def score_tiles(
    slab_field, templ_real, templ_imag, template_norm, cosine_table, sine_table, band_sum, box_edge
):
    planes = slab_field.shape[1]
    field_real, field_imag = forward_two(slab_field, cosine_table, sine_table)
    left_real = field_real.astype(jnp.float32)[:, None]
    left_imag = field_imag.astype(jnp.float32)[:, None]
    right_real = templ_real.astype(jnp.float32)[None]
    right_imag = templ_imag.astype(jnp.float32)[None]
    prod_real = jnp.sum(left_real * right_real + left_imag * right_imag, axis=2).astype(
        jnp.bfloat16
    )
    prod_imag = jnp.sum(left_imag * right_real - left_real * right_imag, axis=2).astype(
        jnp.bfloat16
    )
    correlation = inverse_real(prod_real, prod_imag, cosine_table, sine_table)
    energy = jnp.sum(jnp.square(slab_field.astype(jnp.float32)), axis=1)
    summed = jnp.einsum(
        "ka,nab,lb->nkl", band_sum, energy, band_sum, precision=lax.Precision.HIGHEST
    )
    local_rms = jnp.sqrt(summed / (box_edge * box_edge * planes) + 1e-05)
    ratio = correlation / (local_rms[:, None] * template_norm[None, :, None, None])
    return jnp.max(ratio, axis=1)


def orient_max(best):
    groups = lax.axis_size("orient")
    parts = lax.all_to_all(best, "orient", split_axis=1, concat_axis=0, tiled=True)
    stacked = parts.reshape(groups, best.shape[0], parts.shape[1], parts.shape[2])
    return jnp.max(stacked, axis=0)


def per_device(tiles, assigned_worker, wedge_mask, template_volume, rotation_samples):
    tile_len = tiles.shape[-1]
    planes = tiles.shape[1]
    home_slots = tiles.shape[0]
    work_slots = home_slots // 2
    box_edge = template_volume.shape[0]
    cosine_table, sine_table = tables(tile_len)
    band_sum = band_table(tile_len, box_edge)
    wedge_weight = wedge_mask.astype(jnp.bfloat16)
    templ_real, templ_imag, template_norm = make_templates(
        template_volume, rotation_samples, box_edge, planes, tile_len, cosine_table, sine_table
    )
    occupied = assigned_worker >= 0
    own_count = jnp.sum(occupied.astype(jnp.int32))
    partner_tiles = partner(tiles[work_slots:], "slab", 0)
    counter = jnp.arange(work_slots, dtype=jnp.int32)
    keep_own = (counter < own_count)[:, None, None, None]
    moved_in = pick_rows(counter - own_count, partner_tiles)
    gathered = jnp.where(keep_own, tiles[:work_slots], moved_in)
    slab_field = filtered(gathered, wedge_weight, cosine_table, sine_table)
    best = score_tiles(
        slab_field,
        templ_real,
        templ_imag,
        template_norm,
        cosine_table,
        sine_table,
        band_sum,
        box_edge,
    )
    best_rows = orient_max(best.astype(jnp.bfloat16))
    outgoing = pick_rows(counter + own_count, best_rows)
    returned = partner(outgoing, "slab", 0)
    result = jnp.concatenate([best_rows, returned], axis=0)
    return jnp.where(occupied[:, None, None], result, jnp.zeros_like(result))


def solution(mesh):
    return jax.shard_map(
        per_device,
        mesh=mesh,
        in_specs=(P("slab", None, None, None), P("slab"), P(), P(), P("orient", "slab")),
        out_specs=P("slab", "orient", None),
        check_vma=False,
    )
```

profile of v0, /device:TPU:0, one launch (start us, length us, event | category | flops | bytes accessed | tf_op | source)
XLA Modules:
  0.0 180.5 jit_solution(15834255213761315557)
XLA Ops:
  0.0 1.8 slice.7
  1.8 2.9 %collective-permute-start = (bf16[12,1,128,128]{3,2,1,0:T(8,128)(2,1)}, bf16[12,1,128,128]{3,2,1,0:T(8,128)(2,1)}, u32[]{:S(2)}, u32[]{:S(2)}) collective-permute-start(bf16[12,1,128,128]{3,2,1,0:T(8,128)(2,1)} %slice.7), channel_id=1, source_target_pairs={{0,4},{4,0},{8,12},{12,8},{16,20},{20,16},{24,28},{28,24},{1,5},{5... | collective-permute-start | bytes 1179656 | tf_op jit(solution)/shard_map/ppermute | solution.py:15
  4.7 1.9 %reshape.192 = bf16[262144]{0:T(1024)(128)(2,1)S(1)} reshape(f32[64,64,64]{2,1,0:T(8,128)} %param.8) | data formatting | bytes 1572864 | tf_op jit(solution)/shard_map/reshape | solution.py:84
  6.6 0.8 fusion.131
  7.4 0.0 copy-start.2
  7.4 50.7 %gather_fusion = bf16[8192]{0:T(1024)(128)(2,1)S(1)} fusion(bf16[262144]{0:T(1024)(128)(2,1)S(1)} %reshape.192, s32[8192]{0:T(1024)S(1)} %broadcast_clamp_fusion), kind=kCustom, calls=%fused_computation | custom fusion | bytes 65536 | tf_op jit(solution)/shard_map/jit(_take)/gather | solution.py:84
  58.1 0.0 copy-done.1
  58.2 30.9 %all_gather.3 = bf16[16,4096]{1,0:T(8,128)(2,1)S(1)} all-gather(bf16[16,512]{1,0:T(8,128)(2,1)S(1)} %select_convert_fusion), channel_id=1, replica_groups=mesh['slab'=8,'orient'=4] {'slab'}, dimensions={1}, use_global_device_ids=true | all-gather | bytes 147456 | tf_op jit(solution)/shard_map/all_gather | solution.py:87
  89.0 0.2 reshape.193
  89.3 0.5 fusion.25
  89.8 0.5 convolution_convert_fusion.2
  90.3 0.5 fusion.103
  90.9 0.5 fusion.107
  91.4 0.5 fusion.40
  92.0 0.0 copy-done.3
  92.0 0.6 convert_reduce_fusion
  92.6 0.6 iota_add_fusion
  93.3 0.5 fusion.43
  93.8 0.7 iota_compare_fusion.4
  94.5 0.3 copy.137
  94.8 0.0 copy-done.2
  94.8 0.1 copy.115
  95.0 0.3 copy.131
  95.3 0.1 multiply_reduce_fusion
  95.5 0.0 collective-permute-done
  95.5 1.0 pad.8
  96.5 0.3 copy.171
  96.9 0.3 convolution_convert_fusion
  97.2 0.1 copy.172
  97.3 1.5 convolution_convert_fusion.4
  98.8 1.5 fusion.29
  100.3 0.5 fusion.120
  100.8 0.5 fusion.116
  101.3 0.5 fusion.54
  101.9 1.4 fusion.118
  103.2 0.5 fusion.56
  103.8 1.4 fusion.113
  105.1 2.9 %fusion.50 = f32[12,128,128]{2,1,0:T(8,128)} fusion(f32[12,128,128]{2,1,0:T(8,128)} %fusion.118, bf16[12,128,128]{1,2,0:T(8,128)(2,1)S(1)} %fusion.56), kind=kOutput, calls=%fused_computation.74 | convolution fusion | flops 101548032 | bytes 1966080 | tf_op jit(solution)/shard_map/ka,...ab->...kb/dot_general | solution.py:37
  108.0 2.2 %fusion.34 = bf16[12,128,128]{2,1,0:T(8,128)(2,1)S(1)} fusion(f32[12,128,128]{2,1,0:T(8,128)} %fusion.50, f32[12,128,128]{2,1,0:T(8,128)} %fusion.113, bf16[12,128,128]{1,2,0:T(8,128)(2,1)S(1)} %fusion.54), kind=kOutput, calls=%fused_computation.56 | convolution fusion | flops 102137856 | bytes 2359296 | tf_op jit(solution)/shard_map/ka,...ab->...kb/dot_general | solution.py:37
  110.2 0.5 fusion.35
  110.7 0.5 convolution_convert_fusion.3
  111.2 1.5 fusion.57
  112.7 0.5 fusion.105
  113.2 1.4 fusion.110
  114.6 1.4 fusion.46
  116.0 1.4 copy.134
  117.4 2.5 %fusion.49 = f32[12,128,128]{1,2,0:T(8,128)} fusion(f32[12,128,128]{2,1,0:T(8,128)} %fusion.110, bf16[12,128,128]{2,1,0:T(8,128)(2,1)S(1)} %fusion.35), kind=kOutput, calls=%fused_computation.73 | convolution fusion | flops 51167232 | bytes 1966080 | tf_op jit(solution)/shard_map/ka,...ab->...kb/dot_general | solution.py:37
  119.9 2.3 %copy.128 = f32[12,128,128]{2,1,0:T(8,128)} copy(f32[12,128,128]{1,2,0:T(8,128)} %fusion.49) | data formatting | bytes 1572864 | tf_op jit(solution)/shard_map/mul | solution.py:106
  122.2 6.9 %fusion.2 = f32[12,16,128,128]{3,2,1,0:T(8,128)} fusion(f32[16,128,128]{2,1,0:T(8,128)S(1)} %copy.137, f32[12,128,128]{2,1,0:T(8,128)S(1)} %copy.134, f32[16,128,128]{2,1,0:T(8,128)S(1)} %copy.131, f32[12,128,128]{2,1,0:T(8,128)} %copy.128), kind=kOutput, calls=%fused_computation.9 | convolution fusion | flops 818135040 | bytes 16252928 | tf_op jit(solution)/shard_map/...ab,bc->...ac/dot_general | solution.py:33
  129.1 0.0 copy-done
  129.1 5.8 %fusion.1 = f32[12,16,128,128]{3,2,1,0:T(8,128)} fusion(f32[16,128,128]{2,1,0:T(8,128)S(1)} %copy.137, f32[12,128,128]{2,1,0:T(8,128)S(1)} %copy.134, f32[16,128,128]{2,1,0:T(8,128)S(1)} %copy.131, f32[12,128,128]{2,1,0:T(8,128)S(1)} %copy-done), kind=kOutput, calls=%fused_computation.8 | convolution fusion | flops 818135040 | bytes 16252928 | tf_op jit(solution)/shard_map/...ab,bc->...ac/dot_general | solution.py:33
  134.9 10.1 %fusion.5 = f32[12,16,128,128]{3,2,1,0:T(8,128)} fusion(f32[12,16,128,128]{3,2,1,0:T(8,128)} %fusion.2, f32[16,128,128]{2,1,0:T(8,128)S(1)} %copy.137, f32[12,128,128]{2,1,0:T(8,128)S(1)} %copy.134, f32[16,128,128]{2,1,0:T(8,128)S(1)} %copy.131, f32[12,128,128]{2,1,0:T(8,128)} %copy.128), kind=kOutput, calls=%fused_computation.12 | convolution fusion | flops 1629978624 | bytes 28835840 | tf_op jit(solution)/shard_map/ka,...ab->...kb/dot_general | solution.py:37
  144.9 2.7 %fusion.27 = f32[12,128,128]{2,1,0:T(8,128)} fusion(f32[12,128,128]{1,2,0:T(8,128)} %fusion.57), kind=kOutput, calls=%fused_computation.40 | convolution fusion | flops 302596096 | bytes 1572864 | tf_op jit(solution)/shard_map/ka,nab,lb->nkl/dot_general | solution.py:114
  147.6 2.3 %copy.141 = f32[12,128,128]{1,2,0:T(8,128)} copy(f32[12,128,128]{2,1,0:T(8,128)} %fusion.27) | data formatting | bytes 1572864 | tf_op jit(solution)/shard_map/sqrt | solution.py:117
  150.0 12.2 %fusion = bf16[12,128,128]{1,2,0:T(8,128)(2,1)S(1)} fusion(f32[12,16,128,128]{3,2,1,0:T(8,128)} %fusion.5, f32[16]{0:T(128)S(1)} %add_sqrt_fusion, f32[12,128,128]{1,2,0:T(8,128)} %copy.141, f32[12,16,128,128]{3,2,1,0:T(8,128)} %fusion.1, f32[16,128,128]{2,1,0:T(8,128)S(1)} %copy.137, f32[12,128,128]{2,1,0:T(8,128)S(1)} %copy.134, ...), kind=kOutput, calls=%fused_computation.7 | convolution fusion | flops 1645510656 | bytes 30015552 | tf_op jit(solution)/shard_map/ka,...ab->...kb/dot_general | solution.py:37
  162.2 0.4 copy.142
  162.6 11.5 %all_to_all.12 = bf16[12,128,128]{2,0,1:T(8,128)(2,1)S(1)} all-to-all(bf16[12,128,128]{2,0,1:T(8,128)(2,1)S(1)} %copy.142), channel_id=1, replica_groups=mesh['slab'=8,'orient'=4] {'orient'}, dimensions={1} | all-to-all | bytes 786432 | tf_op jit(solution)/shard_map/all_to_all | solution.py:124
  174.1 0.1 reduce_max.19
  174.2 0.1 copy.174
  174.3 0.2 convolution_convert_fusion.1
  174.6 0.6 collective-permute-start.1
  175.2 4.4 %collective-permute-done.1 = bf16[12,32,128]{2,0,1:T(8,128)(2,1)S(1)} collective-permute-done((bf16[12,32,128]{2,0,1:T(8,128)(2,1)S(1)}, bf16[12,32,128]{2,0,1:T(8,128)(2,1)S(1)}, u32[]{:S(2)}, u32[]{:S(2)}) %collective-permute-start.1) | collective-permute-done | bytes 98336 | tf_op jit(solution)/shard_map/ppermute | solution.py:15
  179.7 0.1 maximum_select_fusion
  179.8 0.7 copy.145
  (15 shorter events, 0.2 us)
Async XLA Ops:
  0.0 58.1 %copy-start.1 = (s32[16,512]{1,0:T(8,128)S(1)}, s32[16,512]{1,0:T(8,128)}, u32[]{:S(2)}) copy-start(s32[16,512]{1,0:T(8,128)} %param.9) | copy-start | bytes 98308
  1.8 93.7 %collective-permute-start = (bf16[12,1,128,128]{3,2,1,0:T(8,128)(2,1)}, bf16[12,1,128,128]{3,2,1,0:T(8,128)(2,1)}, u32[]{:S(2)}, u32[]{:S(2)}) collective-permute-start(bf16[12,1,128,128]{3,2,1,0:T(8,128)(2,1)} %slice.7), channel_id=1, source_target_pairs={{0,4},{4,0},{8,12},{12,8},{16,20},{20,16},{24,28},{28,24},{1,5},{5... | collective-permute-start | bytes 1179656 | tf_op jit(solution)/shard_map/ppermute | solution.py:15
  7.3 84.6 %copy-start.3 = (s32[24]{0:T(128)S(1)}, s32[24]{0:T(128)}, u32[]{:S(2)}) copy-start(s32[24]{0:T(128)} %param.6) | copy-start | bytes 292
  7.4 87.4 %copy-start.2 = (s32[128,128]{1,0:T(8,128)S(1)}, s32[128,128]{1,0:T(8,128)}, u32[]{:S(2)}) copy-start(s32[128,128]{1,0:T(8,128)} %param.7) | copy-start | bytes 196612
  122.2 6.9 %copy-start = (f32[12,128,128]{2,1,0:T(8,128)S(1)}, f32[12,128,128]{2,1,0:T(8,128)}, u32[]{:S(2)}) copy-start(f32[12,128,128]{2,1,0:T(8,128)} %copy.128) | copy-start | bytes 2359300
  174.6 5.0 %collective-permute-start.1 = (bf16[12,32,128]{2,0,1:T(8,128)(2,1)S(1)}, bf16[12,32,128]{2,0,1:T(8,128)(2,1)S(1)}, u32[]{:S(2)}, u32[]{:S(2)}) collective-permute-start(bf16[12,32,128]{2,0,1:T(8,128)(2,1)S(1)} %copy.144), channel_id=1, source_target_pairs={{0,4},{4,0},{8,12},{12,8},{16,20},{20,16},{24,28},{28,24},{1,5},{5... | collective-permute-start | bytes 294920 | tf_op jit(solution)/shard_map/ppermute | solution.py:15
where the time goes:
time: 181 us; the launch traced here: 180 us
  local copies, waits for them, and re-layouts  64.2 us (35%)
  matrix products  62.5 us (35%)
  blocking collectives  42.3 us (23%)
  waiting for transfers between devices  4.44 us (2%)
  starting transfers between devices  3.53 us (2%)
  other arithmetic  3.09 us (2%)
    gather x2, local copies, waits for them, and re-layouts, make_templates(): jnp.take(template_volume.reshape(-1), rotation_samples, axis=0)  50.7 us
    dot_general x16, matrix products, left_mul(): jnp.einsum('ka,...ab->...kb', table, values, preferred_element_type=jnp.f...  37.3 us
    all_gather x1, blocking collectives, make_templates(): sampled = lax.all_gather(sampled_part, 'slab', axis=1, tiled=True)  30.9 us
    dot_general x10, matrix products, right_mul(): jnp.einsum('...ab,bc->...ac', values, table, preferred_element_type=jnp.f...  20.4 us
    all_to_all x1, blocking collectives, orient_max(): lax.all_to_all(best, 'orient', split_axis=1, concat_axis=0, tiled=True)  11.5 us
    ppermute x2, waiting for transfers between devices, partner(): return lax.ppermute(block, axis, route)  4.44 us
    dot_general x2, matrix products, score_tiles(): jnp.einsum('ka,nab,lb->nkl', band_sum, energy, band_sum, precision=lax.Pr...  4.21 us
  transfers between devices with their start and end apart: 2, of which 1 were waited for; matrix products, arithmetic and copies ran while one was open for 33% of the time, Pallas kernels for 0%

commit v1 on v0

--- a/solution.py
+++ b/solution.py
@@ -3,6 +3,27 @@
 import jax.numpy as jnp
 from jax import lax
 from jax.sharding import PartitionSpec as P
+
+
+def gather_around(shard, axis, dim):
+    size, place, width = (lax.axis_size(axis), lax.axis_index(axis), shard.shape[dim])
+    right = [(i, (i + 1) % size) for i in range(size)]
+    left = [(i, (i - 1) % size) for i in range(size)]
+    result = jnp.zeros((*shard.shape[:dim], size * width, *shard.shape[dim + 1 :]), shard.dtype)
+    result = lax.dynamic_update_slice_in_dim(result, shard, place * width, axis=dim)
+    from_left = from_right = shard
+    half = size // 2
+    for step in range(1, half + 1):
+        from_left = lax.ppermute(from_left, axis, right)
+        result = lax.dynamic_update_slice_in_dim(
+            result, from_left, (place - step) % size * width, axis=dim
+        )
+        if step < size - half:
+            from_right = lax.ppermute(from_right, axis, left)
+            result = lax.dynamic_update_slice_in_dim(
+                result, from_right, (place + step) % size * width, axis=dim
+            )
+    return result
 
 
 def partner(block, axis, bit):
@@ -84,7 +105,7 @@
     sampled_part = jnp.take(template_volume.reshape(-1), rotation_samples, axis=0).astype(
         jnp.bfloat16
     )
-    sampled = lax.all_gather(sampled_part, "slab", axis=1, tiled=True)
+    sampled = gather_around(sampled_part, "slab", 1)
     sampled = sampled.reshape(count, planes, box_edge, box_edge)
     padded = jnp.pad(sampled, ((0, 0), (0, 0), (0, tile_len - box_edge), (0, tile_len - box_edge)))
     template_norm = jnp.sqrt(

time: 181 us -> 173 us (0.956)
  blocking collectives: 42.3 us -> 11.4 us
  starting transfers between devices: 3.53 us -> 15.7 us
  waiting for transfers between devices: 4.44 us -> 15.3 us
    all_gather x1 -> x0, blocking collectives: 30.9 us -> none  [make_templates(): sampled = lax.all_gather(sampled_part, 'slab', axis=1, tiled=True)]
    ppermute x0 -> x7, starting transfers between devices: none -> 15.6 us  [the longest x3 8.05 us: gather_around(): from_right = lax.ppermute(from_right, axis, left)]
    ppermute x0 -> x7, waiting for transfers between devices: none -> 10.4 us  [the longest x4 10.4 us: gather_around(): from_left = lax.ppermute(from_left, axis, right)]
    ppermute x2, starting transfers between devices: 3.53 us -> 0.07 us  [partner(): return lax.ppermute(block, axis, route)]
  transfers between devices with their start and end apart: 2 -> 9, of which waited for: 1 -> 4; matrix products, arithmetic and copies ran while one was open for 33% -> 4% of each run, Pallas kernels for 0% -> 0%
where the time goes in v1:
time: 173 us; the launch traced here: 172 us
  local copies, waits for them, and re-layouts  63.4 us (37%)
  matrix products  62.9 us (36%)
  starting transfers between devices  15.7 us (9%)
  waiting for transfers between devices  15.3 us (9%)
  blocking collectives  11.4 us (7%)
  other arithmetic  3.1 us (2%)
    gather x2, local copies, waits for them, and re-layouts, make_templates(): jnp.take(template_volume.reshape(-1), rotation_samples, axis=0)  50.7 us
    dot_general x16, matrix products, left_mul(): jnp.einsum('ka,...ab->...kb', table, values, preferred_element_type=jnp.f...  37.5 us
    dot_general x10, matrix products, right_mul(): jnp.einsum('...ab,bc->...ac', values, table, preferred_element_type=jnp.f...  20.7 us
    all_to_all x1, blocking collectives, orient_max(): lax.all_to_all(best, 'orient', split_axis=1, concat_axis=0, tiled=True)  11.4 us
    ppermute x4, waiting for transfers between devices, gather_around(): from_left = lax.ppermute(from_left, axis, right)  10.4 us
    ppermute x3, starting transfers between devices, gather_around(): from_right = lax.ppermute(from_right, axis, left)  8.05 us
    ppermute x4, starting transfers between devices, gather_around(): from_left = lax.ppermute(from_left, axis, right)  7.57 us
    ppermute x2, waiting for transfers between devices, partner(): return lax.ppermute(block, axis, route)  4.94 us
  transfers between devices with their start and end apart: 9, of which 4 were waited for; matrix products, arithmetic and copies ran while one was open for 4% of the time, Pallas kernels for 0%

profile of v1, /device:TPU:0, one launch (start us, length us, event | category | flops | bytes accessed | tf_op | source)
XLA Modules:
  0.0 172.3 jit_solution(15229183943070690743)
XLA Ops:
  0.0 1.9 %reshape.192 = bf16[262144]{0:T(1024)(128)(2,1)S(1)} reshape(f32[64,64,64]{2,1,0:T(8,128)} %param.8) | data formatting | bytes 1572864 | tf_op jit(solution)/shard_map/reshape | solution.py:105
  2.0 0.8 fusion.131
  2.8 50.7 %gather_fusion = bf16[8192]{0:T(1024)(128)(2,1)S(1)} fusion(bf16[262144]{0:T(1024)(128)(2,1)S(1)} %reshape.192, s32[8192]{0:T(1024)S(1)} %broadcast_clamp_fusion), kind=kCustom, calls=%fused_computation | custom fusion | bytes 65536 | tf_op jit(solution)/shard_map/jit(_take)/gather | solution.py:105
  53.6 3.0 %collective-permute-start.1 = (bf16[16,512]{1,0:T(8,128)(2,1)S(1)}, bf16[16,512]{1,0:T(8,128)(2,1)S(1)}, u32[]{:S(2)}, u32[]{:S(2)}) collective-permute-start(bf16[16,512]{1,0:T(8,128)(2,1)S(1)} %get-tuple-element.6), channel_id=1, source_target_pairs={{0,4},{4,8},{8,12},{12,16},{16,20},{20,24},{24,28},{28,0},{1,5},{5... | collective-permute-start | bytes 49160 | tf_op jit(solution)/shard_map/ppermute | solution.py:17
  56.6 3.1 %collective-permute-start.2 = (bf16[16,512]{1,0:T(8,128)(2,1)S(1)}, bf16[16,512]{1,0:T(8,128)(2,1)S(1)}, u32[]{:S(2)}, u32[]{:S(2)}) collective-permute-start(bf16[16,512]{1,0:T(8,128)(2,1)S(1)} %get-tuple-element.6), channel_id=1, source_target_pairs={{0,28},{4,0},{8,4},{12,8},{16,12},{20,16},{24,20},{28,24},{1,29},{... | collective-permute-start | bytes 49160 | tf_op jit(solution)/shard_map/ppermute | solution.py:22
  59.7 0.8 slice.7
  60.5 0.6 convert_reduce_fusion
  61.1 0.6 iota_add_fusion
  61.8 0.7 iota_compare_fusion.4
  62.6 0.1 copy.115
  62.7 2.1 %collective-permute-start.3 = (bf16[16,512]{1,0:T(8,128)(2,1)S(1)}, bf16[16,512]{1,0:T(8,128)(2,1)S(1)}, u32[]{:S(2)}, u32[]{:S(2)}) collective-permute-start(bf16[16,512]{1,0:T(8,128)(2,1)S(1)} %collective-permute-done.1), channel_id=1, source_target_pairs={{0,4},{4,8},{8,12},{12,16},{16,20},{20,24},{24,28},{28,0},{1,5},{5... | collective-permute-start | bytes 49160 | tf_op jit(solution)/shard_map/ppermute | solution.py:17
  64.8 2.7 %collective-permute-start.4 = (bf16[16,512]{1,0:T(8,128)(2,1)S(1)}, bf16[16,512]{1,0:T(8,128)(2,1)S(1)}, u32[]{:S(2)}, u32[]{:S(2)}) collective-permute-start(bf16[16,512]{1,0:T(8,128)(2,1)S(1)} %collective-permute-done.2), channel_id=1, source_target_pairs={{0,28},{4,0},{8,4},{12,8},{16,12},{20,16},{24,20},{28,24},{1,29},{... | collective-permute-start | bytes 49160 | tf_op jit(solution)/shard_map/ppermute | solution.py:22
  67.5 2.2 %collective-permute-done.3 = bf16[16,512]{1,0:T(8,128)(2,1)S(1)} collective-permute-done((bf16[16,512]{1,0:T(8,128)(2,1)S(1)}, bf16[16,512]{1,0:T(8,128)(2,1)S(1)}, u32[]{:S(2)}, u32[]{:S(2)}) %collective-permute-start.3) | collective-permute-done | bytes 16416 | tf_op jit(solution)/shard_map/ppermute | solution.py:17
  69.7 2.5 %collective-permute-start.5 = (bf16[16,512]{1,0:T(8,128)(2,1)S(1)}, bf16[16,512]{1,0:T(8,128)(2,1)S(1)}, u32[]{:S(2)}, u32[]{:S(2)}) collective-permute-start(bf16[16,512]{1,0:T(8,128)(2,1)S(1)} %collective-permute-done.3), channel_id=1, source_target_pairs={{0,4},{4,8},{8,12},{12,16},{16,20},{20,24},{24,28},{28,0},{1,5},{5... | collective-permute-start | bytes 49160 | tf_op jit(solution)/shard_map/ppermute | solution.py:17
  72.2 2.2 %collective-permute-start.6 = (bf16[16,512]{1,0:T(8,128)(2,1)S(1)}, bf16[16,512]{1,0:T(8,128)(2,1)S(1)}, u32[]{:S(2)}, u32[]{:S(2)}) collective-permute-start(bf16[16,512]{1,0:T(8,128)(2,1)S(1)} %collective-permute-done.4), channel_id=1, source_target_pairs={{0,28},{4,0},{8,4},{12,8},{16,12},{20,16},{24,20},{28,24},{1,29},{... | collective-permute-start | bytes 49160 | tf_op jit(solution)/shard_map/ppermute | solution.py:22
  74.5 1.7 collective-permute-done.5
  76.2 6.4 %collective-permute-done.7 = bf16[16,512]{1,0:T(8,128)(2,1)S(1)} collective-permute-done((bf16[16,512]{1,0:T(8,128)(2,1)S(1)}, bf16[16,512]{1,0:T(8,128)(2,1)S(1)}, u32[]{:S(2)}, u32[]{:S(2)}) %collective-permute-start.7) | collective-permute-done | bytes 16416 | tf_op jit(solution)/shard_map/ppermute | solution.py:17
  82.6 0.2 reshape.193
  82.9 0.5 fusion.25
  83.4 0.5 convolution_convert_fusion.2
  83.9 0.5 fusion.103
  84.5 0.5 fusion.107
  85.0 0.5 fusion.40
  85.6 0.5 fusion.43
  86.1 0.3 copy.137
  86.5 0.3 copy.131
  86.8 0.1 multiply_reduce_fusion
  87.0 1.0 pad.8
  88.0 0.3 copy.171
  88.4 0.3 convolution_convert_fusion
  88.7 0.1 copy.172
  88.8 1.5 convolution_convert_fusion.4
  90.3 1.5 fusion.29
  91.8 0.5 fusion.120
  92.3 0.5 fusion.116
  92.8 0.5 fusion.54
  93.3 1.4 fusion.118
  94.7 0.5 fusion.56
  95.2 1.4 fusion.113
  96.7 2.8 %fusion.50 = f32[12,128,128]{2,1,0:T(8,128)} fusion(f32[12,128,128]{2,1,0:T(8,128)} %fusion.118, bf16[12,128,128]{1,2,0:T(8,128)(2,1)S(1)} %fusion.56), kind=kOutput, calls=%fused_computation.74 | convolution fusion | flops 101548032 | bytes 1966080 | tf_op jit(solution)/shard_map/ka,...ab->...kb/dot_general | solution.py:58
  99.5 2.2 %fusion.34 = bf16[12,128,128]{2,1,0:T(8,128)(2,1)S(1)} fusion(f32[12,128,128]{2,1,0:T(8,128)} %fusion.50, f32[12,128,128]{2,1,0:T(8,128)} %fusion.113, bf16[12,128,128]{1,2,0:T(8,128)(2,1)S(1)} %fusion.54), kind=kOutput, calls=%fused_computation.56 | convolution fusion | flops 102137856 | bytes 2359296 | tf_op jit(solution)/shard_map/ka,...ab->...kb/dot_general | solution.py:58
  101.7 0.5 fusion.35
  102.2 0.5 convolution_convert_fusion.3
  102.7 1.5 fusion.57
  104.2 0.5 fusion.105
  104.7 1.4 fusion.110
  106.1 1.4 fusion.46
  107.5 1.4 copy.134
  108.9 2.7 %fusion.49 = f32[12,128,128]{1,2,0:T(8,128)} fusion(f32[12,128,128]{2,1,0:T(8,128)} %fusion.110, bf16[12,128,128]{2,1,0:T(8,128)(2,1)S(1)} %fusion.35), kind=kOutput, calls=%fused_computation.73 | convolution fusion | flops 51167232 | bytes 1966080 | tf_op jit(solution)/shard_map/ka,...ab->...kb/dot_general | solution.py:58
  111.6 2.3 %copy.128 = f32[12,128,128]{2,1,0:T(8,128)} copy(f32[12,128,128]{1,2,0:T(8,128)} %fusion.49) | data formatting | bytes 1572864 | tf_op jit(solution)/shard_map/mul | solution.py:127
  113.9 7.0 %fusion.2 = f32[12,16,128,128]{3,2,1,0:T(8,128)} fusion(f32[16,128,128]{2,1,0:T(8,128)S(1)} %copy.137, f32[12,128,128]{2,1,0:T(8,128)S(1)} %copy.134, f32[16,128,128]{2,1,0:T(8,128)S(1)} %copy.131, f32[12,128,128]{2,1,0:T(8,128)} %copy.128), kind=kOutput, calls=%fused_computation.9 | convolution fusion | flops 818135040 | bytes 16252928 | tf_op jit(solution)/shard_map/...ab,bc->...ac/dot_general | solution.py:54
  120.9 5.8 %fusion.1 = f32[12,16,128,128]{3,2,1,0:T(8,128)} fusion(f32[16,128,128]{2,1,0:T(8,128)S(1)} %copy.137, f32[12,128,128]{2,1,0:T(8,128)S(1)} %copy.134, f32[16,128,128]{2,1,0:T(8,128)S(1)} %copy.131, f32[12,128,128]{2,1,0:T(8,128)S(1)} %copy-done), kind=kOutput, calls=%fused_computation.8 | convolution fusion | flops 818135040 | bytes 16252928 | tf_op jit(solution)/shard_map/...ab,bc->...ac/dot_general | solution.py:54
  126.8 10.1 %fusion.5 = f32[12,16,128,128]{3,2,1,0:T(8,128)} fusion(f32[12,16,128,128]{3,2,1,0:T(8,128)} %fusion.2, f32[16,128,128]{2,1,0:T(8,128)S(1)} %copy.137, f32[12,128,128]{2,1,0:T(8,128)S(1)} %copy.134, f32[16,128,128]{2,1,0:T(8,128)S(1)} %copy.131, f32[12,128,128]{2,1,0:T(8,128)} %copy.128), kind=kOutput, calls=%fused_computation.12 | convolution fusion | flops 1629978624 | bytes 28835840 | tf_op jit(solution)/shard_map/ka,...ab->...kb/dot_general | solution.py:58
  136.8 2.7 %fusion.27 = f32[12,128,128]{2,1,0:T(8,128)} fusion(f32[12,128,128]{1,2,0:T(8,128)} %fusion.57), kind=kOutput, calls=%fused_computation.40 | convolution fusion | flops 302596096 | bytes 1572864 | tf_op jit(solution)/shard_map/ka,nab,lb->nkl/dot_general | solution.py:135
  139.5 2.3 %copy.141 = f32[12,128,128]{1,2,0:T(8,128)} copy(f32[12,128,128]{2,1,0:T(8,128)} %fusion.27) | data formatting | bytes 1572864 | tf_op jit(solution)/shard_map/sqrt | solution.py:138
  141.8 12.2 %fusion = bf16[12,128,128]{1,2,0:T(8,128)(2,1)S(1)} fusion(f32[12,16,128,128]{3,2,1,0:T(8,128)} %fusion.5, f32[16]{0:T(128)S(1)} %add_sqrt_fusion, f32[12,128,128]{1,2,0:T(8,128)} %copy.141, f32[12,16,128,128]{3,2,1,0:T(8,128)} %fusion.1, f32[16,128,128]{2,1,0:T(8,128)S(1)} %copy.137, f32[12,128,128]{2,1,0:T(8,128)S(1)} %copy.134, ...), kind=kOutput, calls=%fused_computation.7 | convolution fusion | flops 1645510656 | bytes 30015552 | tf_op jit(solution)/shard_map/ka,...ab->...kb/dot_general | solution.py:58
  154.0 0.4 copy.142
  154.5 11.4 %all_to_all.12 = bf16[12,128,128]{2,0,1:T(8,128)(2,1)S(1)} all-to-all(bf16[12,128,128]{2,0,1:T(8,128)(2,1)S(1)} %copy.142), channel_id=1, replica_groups=mesh['slab'=8,'orient'=4] {'orient'}, dimensions={1} | all-to-all | bytes 786432 | tf_op jit(solution)/shard_map/all_to_all | solution.py:145
  165.9 0.1 reduce_max.19
  166.1 0.2 convolution_convert_fusion.1
  166.5 0.1 collective-permute-start.8
  166.6 4.9 %collective-permute-done.8 = bf16[12,32,128]{2,0,1:T(8,128)(2,1)S(1)} collective-permute-done((bf16[12,32,128]{2,0,1:T(8,128)(2,1)S(1)}, bf16[12,32,128]{2,0,1:T(8,128)(2,1)S(1)}, u32[]{:S(2)}, u32[]{:S(2)}) %collective-permute-start.8) | collective-permute-done | bytes 98336 | tf_op jit(solution)/shard_map/ppermute | solution.py:36
  171.5 0.1 maximum_select_fusion
  171.6 0.7 copy.145
  (38 shorter events, 0.3 us)
Async XLA Ops:
  0.0 53.5 %copy-start.2 = (s32[16,512]{1,0:T(8,128)S(1)}, s32[16,512]{1,0:T(8,128)}, u32[]{:S(2)}) copy-start(s32[16,512]{1,0:T(8,128)} %param.9) | copy-start | bytes 98308
  0.0 59.7 %copy-start.1 = (bf16[24,1,128,128]{3,2,1,0:T(8,128)(2,1)S(1)}, bf16[24,1,128,128]{3,2,1,0:T(8,128)(2,1)}, u32[]{:S(2)}) copy-start(bf16[24,1,128,128]{3,2,1,0:T(8,128)(2,1)} %param.5) | copy-start | bytes 2359300
  0.0 60.5 %copy-start.4 = (s32[24]{0:T(128)S(1)}, s32[24]{0:T(128)}, u32[]{:S(2)}) copy-start(s32[24]{0:T(128)} %param.6) | copy-start | bytes 292
  0.0 62.5 %copy-start.3 = (s32[128,128]{1,0:T(8,128)S(1)}, s32[128,128]{1,0:T(8,128)}, u32[]{:S(2)}) copy-start(s32[128,128]{1,0:T(8,128)} %param.7) | copy-start | bytes 196612
  53.6 9.1 %collective-permute-start.1 = (bf16[16,512]{1,0:T(8,128)(2,1)S(1)}, bf16[16,512]{1,0:T(8,128)(2,1)S(1)}, u32[]{:S(2)}, u32[]{:S(2)}) collective-permute-start(bf16[16,512]{1,0:T(8,128)(2,1)S(1)} %get-tuple-element.6), channel_id=1, source_target_pairs={{0,4},{4,8},{8,12},{12,16},{16,20},{20,24},{24,28},{28,0},{1,5},{5... | collective-permute-start | bytes 49160 | tf_op jit(solution)/shard_map/ppermute | solution.py:17
  56.6 8.2 %collective-permute-start.2 = (bf16[16,512]{1,0:T(8,128)(2,1)S(1)}, bf16[16,512]{1,0:T(8,128)(2,1)S(1)}, u32[]{:S(2)}, u32[]{:S(2)}) collective-permute-start(bf16[16,512]{1,0:T(8,128)(2,1)S(1)} %get-tuple-element.6), channel_id=1, source_target_pairs={{0,28},{4,0},{8,4},{12,8},{16,12},{20,16},{24,20},{28,24},{1,29},{... | collective-permute-start | bytes 49160 | tf_op jit(solution)/shard_map/ppermute | solution.py:22
  60.5 26.5 %collective-permute-start = (bf16[12,1,128,128]{3,2,1,0:T(8,128)(2,1)}, bf16[12,1,128,128]{3,2,1,0:T(8,128)(2,1)}, u32[]{:S(2)}, u32[]{:S(2)}) collective-permute-start(bf16[12,1,128,128]{3,2,1,0:T(8,128)(2,1)} %slice.7), channel_id=1, source_target_pairs={{0,4},{4,0},{8,12},{12,8},{16,20},{20,16},{24,28},{28,24},{1,5},{5... | collective-permute-start | bytes 1179656 | tf_op jit(solution)/shard_map/ppermute | solution.py:36
  62.7 7.0 %collective-permute-start.3 = (bf16[16,512]{1,0:T(8,128)(2,1)S(1)}, bf16[16,512]{1,0:T(8,128)(2,1)S(1)}, u32[]{:S(2)}, u32[]{:S(2)}) collective-permute-start(bf16[16,512]{1,0:T(8,128)(2,1)S(1)} %collective-permute-done.1), channel_id=1, source_target_pairs={{0,4},{4,8},{8,12},{12,16},{16,20},{20,24},{24,28},{28,0},{1,5},{5... | collective-permute-start | bytes 49160 | tf_op jit(solution)/shard_map/ppermute | solution.py:17
  64.8 7.4 %collective-permute-start.4 = (bf16[16,512]{1,0:T(8,128)(2,1)S(1)}, bf16[16,512]{1,0:T(8,128)(2,1)S(1)}, u32[]{:S(2)}, u32[]{:S(2)}) collective-permute-start(bf16[16,512]{1,0:T(8,128)(2,1)S(1)} %collective-permute-done.2), channel_id=1, source_target_pairs={{0,28},{4,0},{8,4},{12,8},{16,12},{20,16},{24,20},{28,24},{1,29},{... | collective-permute-start | bytes 49160 | tf_op jit(solution)/shard_map/ppermute | solution.py:22
  69.7 6.4 %collective-permute-start.5 = (bf16[16,512]{1,0:T(8,128)(2,1)S(1)}, bf16[16,512]{1,0:T(8,128)(2,1)S(1)}, u32[]{:S(2)}, u32[]{:S(2)}) collective-permute-start(bf16[16,512]{1,0:T(8,128)(2,1)S(1)} %collective-permute-done.3), channel_id=1, source_target_pairs={{0,4},{4,8},{8,12},{12,16},{16,20},{20,24},{24,28},{28,0},{1,5},{5... | collective-permute-start | bytes 49160 | tf_op jit(solution)/shard_map/ppermute | solution.py:17
  72.2 4.0 %collective-permute-start.6 = (bf16[16,512]{1,0:T(8,128)(2,1)S(1)}, bf16[16,512]{1,0:T(8,128)(2,1)S(1)}, u32[]{:S(2)}, u32[]{:S(2)}) collective-permute-start(bf16[16,512]{1,0:T(8,128)(2,1)S(1)} %collective-permute-done.4), channel_id=1, source_target_pairs={{0,28},{4,0},{8,4},{12,8},{16,12},{20,16},{24,20},{28,24},{1,29},{... | collective-permute-start | bytes 49160 | tf_op jit(solution)/shard_map/ppermute | solution.py:22
  76.2 6.4 %collective-permute-start.7 = (bf16[16,512]{1,0:T(8,128)(2,1)S(1)}, bf16[16,512]{1,0:T(8,128)(2,1)S(1)}, u32[]{:S(2)}, u32[]{:S(2)}) collective-permute-start(bf16[16,512]{1,0:T(8,128)(2,1)S(1)} %collective-permute-done.5), channel_id=1, source_target_pairs={{0,4},{4,8},{8,12},{12,16},{16,20},{20,24},{24,28},{28,0},{1,5},{5... | collective-permute-start | bytes 49160 | tf_op jit(solution)/shard_map/ppermute | solution.py:17
  113.9 7.0 %copy-start = (f32[12,128,128]{2,1,0:T(8,128)S(1)}, f32[12,128,128]{2,1,0:T(8,128)}, u32[]{:S(2)}) copy-start(f32[12,128,128]{2,1,0:T(8,128)} %copy.128) | copy-start | bytes 2359300
  166.5 5.0 %collective-permute-start.8 = (bf16[12,32,128]{2,0,1:T(8,128)(2,1)S(1)}, bf16[12,32,128]{2,0,1:T(8,128)(2,1)S(1)}, u32[]{:S(2)}, u32[]{:S(2)}) collective-permute-start(bf16[12,32,128]{2,0,1:T(8,128)(2,1)S(1)} %copy.144), channel_id=1, source_target_pairs={{0,4},{4,0},{8,12},{12,8},{16,20},{20,16},{24,28},{28,24},{1,5},{5... | collective-permute-start | bytes 294920 | tf_op jit(solution)/shard_map/ppermute | solution.py:36
